TPU v7x, 512 devices: a whole 4x4x16 slice. The times are simulated.
512 devices in a mesh: lon: 32 (over z, y_lo), lat: 16 (over y_hi, x, core).
Axes of the slice: x: 4, y: 4 (y_hi: 2, y_lo: 2; y = y_hi * 2 + y_lo), z: 16, core: 2. Of those that a mesh axis runs over, the one named last changes fastest.
Arguments:
- field: bfloat16 [2, 128, 128, 4096], P(None, 'lat', None, 'lon'), may hold values from -6 to 6
- weights: bfloat16 [2, 9, 128, 128], replicated, may hold values from -0.5 to 0.5
- coefs: bfloat16 [4, 128, 9, 4096], P(None, 'lat', None, 'lon'), may hold values from -2 to 2
- land_mask: int32 [2, 128, 4096], P(None, 'lat', 'lon'), may hold values 0 or 1
- fold_flag: int32 [128], replicated, may hold values from 0 to 1
Outputs:
- forward: bfloat16 [2, 128, 128, 4096], P(None, 'lat', None, 'lon')
- adjoint: bfloat16 [2, 128, 128, 4096], P(None, 'lat', None, 'lon')
Inputs may be any that keep to these rules, and one draw needn't show every extreme that they name: `land_mask`: 1 marks an ocean cell, 0 land. `fold_flag`: 1 marks a channel that holds a vector component, which changes sign across the north fold.
All inputs are finite; a program needn't handle non-finite values. No bound on the sum of `land_mask` on one device may be relied on, other than what follows from the above.
Results may differ from a plain program's by a relative error of at most 0.007.
Values may be sent and summed in bfloat16 or wider, within the bound.
No kernel may reach another device: no remote copies, remote signals or barrier semaphores. Data moves between devices by JAX's collectives and lax.ppermute only.
A program may use at most 64 MiB of HBM per device.

v0:
```python
import functools

import jax
import jax.numpy as jnp
from jax import lax
from jax.experimental import pallas as pl
from jax.experimental.pallas import tpu as pltpu
from jax.sharding import PartitionSpec as P

HALO = 4
PAD = 8


def exchange(block, block_in, fold_sign, taps, layers, channels):
    rows = block.shape[1]
    cols = block.shape[2]
    nlon = lax.axis_size("lon")
    nlat = lax.axis_size("lat")
    to_right = [(i, (i + 1) % nlon) for i in range(nlon)]
    to_left = [((i + 1) % nlon, i) for i in range(nlon)]
    from_left = lax.ppermute(block[:, :, cols - HALO :], "lon", to_right)
    from_right = lax.ppermute(block[:, :, :HALO], "lon", to_left)

    top = nlat - 1
    top_rows = block[:, rows - HALO :]

    def across(piece, shift):
        pairs = [(b * nlat + top, ((shift - b) % nlon) * nlat + top) for b in range(nlon)]
        return lax.ppermute(piece, ("lon", "lat"), pairs)

    mirror_low = across(top_rows[:, :, cols - HALO :], nlon - 2)
    mirror_mid = across(block_in[:, rows - HALO :], nlon - 1).transpose(0, 1, 3, 2)
    mirror_high = across(top_rows[:, :, :HALO], nlon)
    mirrored = jnp.concatenate([mirror_low, mirror_mid, mirror_high], axis=2)
    wide = jnp.concatenate([from_left, block, from_right], axis=2)

    to_up = [(j, j + 1) for j in range(nlat - 1)]
    to_down = [(j + 1, j) for j in range(nlat - 1)]
    below = lax.ppermute(wide[:, rows - HALO :], "lat", to_up)
    above = lax.ppermute(wide[:, :HALO], "lat", to_down)
    mirrored = mirrored[:, ::-1, ::-1]
    field_part = mirrored[..., :channels] * fold_sign
    coef_part = mirrored[..., channels : channels + layers * taps]
    coef_part = coef_part.reshape(coef_part.shape[:3] + (layers, taps))[..., ::-1].reshape(
        coef_part.shape
    )
    rest = mirrored[..., channels + layers * taps :]
    mirrored = jnp.concatenate([field_part, coef_part, rest], axis=3)
    is_top = lax.axis_index("lat") == top
    above = jnp.where(is_top, mirrored, above)
    return jnp.concatenate([below, wide, above], axis=1)


def apply_layer(x_ref, aux_ref, w_ref, o_ref, acc_ref, lev, row_lo, row_hi, coef_lane, mask_lane, split, adjoint, mg_ref=None):
    out_cols = acc_ref.shape[1]
    chans = acc_ref.shape[2]
    acc_ref[...] = jnp.zeros(acc_ref.shape, acc_ref.dtype)
    if adjoint:
        src_rows = slice(row_lo - 1, row_hi + 1)
        mg_ref[src_rows] = x_ref[lev, src_rows] * aux_ref[lev, src_rows, :, pl.ds(mask_lane, 1)]
    for tap in range(w_ref.shape[1]):
        dj, di = tap // 3 - 1, tap % 3 - 1
        step = -dj if adjoint else dj
        col = PAD - di if adjoint else PAD + di
        if adjoint:
            groups = ((row_lo, min(row_hi, split + dj), 0), (max(row_lo, split + dj), row_hi, 1))
        else:
            groups = ((row_lo, min(row_hi, split), 0), (max(row_lo, split), row_hi, 1))
        for lo, hi, sel in groups:
            if hi <= lo:
                continue
            count = hi - lo
            src = slice(lo + step, hi + step)
            if adjoint:
                xin = mg_ref[src, pl.ds(col, out_cols), :].reshape(count * out_cols, chans)
                cf = aux_ref[lev, src, pl.ds(col, out_cols), pl.ds(coef_lane + tap, 1)]
                prod = jnp.dot(
                    xin.astype(jnp.bfloat16), w_ref[sel, tap], preferred_element_type=jnp.float32
                )
            else:
                xin = x_ref[lev, src, pl.ds(col, out_cols), :].reshape(count * out_cols, chans)
                cf = aux_ref[lev, lo:hi, pl.ds(PAD, out_cols), pl.ds(coef_lane + tap, 1)]
                prod = lax.dot_general(
                    xin.astype(jnp.bfloat16),
                    w_ref[sel, tap],
                    (((1,), (1,)), ((), ())),
                    preferred_element_type=jnp.float32,
                )
            term = cf.reshape(count * out_cols, 1) * prod
            acc_ref[lo:hi] += term.reshape(count, out_cols, chans)
    result = acc_ref[row_lo:row_hi]
    if not adjoint:
        result = result * aux_ref[lev, row_lo:row_hi, pl.ds(PAD, out_cols), pl.ds(mask_lane, 1)]
    o_ref[lev, row_lo:row_hi, pl.ds(PAD, out_cols), :] = result.astype(jnp.bfloat16).astype(jnp.float32)


def model_kernel(blk_ref, w_ref, fwd_ref, adj_ref, ext_ref, aux_ref, x1_ref, x2_ref, g1_ref, acc_ref, mg_ref, *, rows, cols, layers, taps, split):
    levels, total_rows = ext_ref.shape[0], ext_ref.shape[1]
    chans = ext_ref.shape[3]
    data_cols = blk_ref.shape[2]
    mask_lane = layers * taps
    for buf in (ext_ref, aux_ref, x1_ref, x2_ref, g1_ref):
        buf[...] = jnp.zeros(buf.shape, buf.dtype)
    for lev in range(levels):
        for j in range(total_rows):
            piece = blk_ref[lev, j].astype(jnp.float32)
            ext_ref[lev, j, pl.ds(PAD, data_cols), :] = piece[:, :chans]
            aux_ref[lev, j, pl.ds(PAD, data_cols), :] = piece[:, chans:]

    def store_transposed(out_ref, src_ref, lev):
        for r in range(rows):
            tile = src_ref[lev, HALO + r, pl.ds(PAD + HALO, cols), :]
            out_ref[lev, r] = jnp.transpose(tile).astype(out_ref.dtype)

    def level_body(lev, carry):
        apply_layer(ext_ref, aux_ref, w_ref.at[0], x1_ref, acc_ref, lev, 1, total_rows - 1, 0, mask_lane, split, False)
        apply_layer(x1_ref, aux_ref, w_ref.at[1], x2_ref, acc_ref, lev, 2, total_rows - 2, taps, mask_lane, split, False)
        store_transposed(fwd_ref, x2_ref, lev)
        apply_layer(x2_ref, aux_ref, w_ref.at[1], g1_ref, acc_ref, lev, 3, total_rows - 3, taps, mask_lane, split, True, mg_ref)
        apply_layer(g1_ref, aux_ref, w_ref.at[0], x1_ref, acc_ref, lev, 4, total_rows - 4, 0, mask_lane, split, True, mg_ref)
        store_transposed(adj_ref, x1_ref, lev)
        return carry

    lax.fori_loop(0, levels, level_body, 0)


def run_model(blk, both, rows, cols, layers, taps, split):
    levels, total_rows, data_cols, lanes = blk.shape
    chans = both.shape[-1]
    width = data_cols + 2 * PAD
    kernel = functools.partial(
        model_kernel, rows=rows, cols=cols, layers=layers, taps=taps, split=split
    )
    out_cols = width - 2 * PAD
    done_rows = sum(total_rows - 2 * k for k in range(1, 2 * layers + 1))
    flops = 2 * levels * done_rows * out_cols * chans * chans * taps
    out = jax.ShapeDtypeStruct((levels, rows, chans, cols), jnp.bfloat16)
    buf = pltpu.VMEM((levels, total_rows, width, chans), jnp.float32)
    return pl.pallas_call(
        kernel,
        out_shape=(out, out),
        in_specs=[pl.BlockSpec(memory_space=pltpu.VMEM)] * 2,
        out_specs=(pl.BlockSpec(memory_space=pltpu.VMEM), pl.BlockSpec(memory_space=pltpu.VMEM)),
        scratch_shapes=[
            buf,
            pltpu.VMEM((levels, total_rows, width, lanes - chans), jnp.float32),
            buf,
            buf,
            buf,
            pltpu.VMEM((total_rows, out_cols, chans), jnp.float32),
            pltpu.VMEM((total_rows, width, chans), jnp.float32),
        ],
        cost_estimate=pl.CostEstimate(
            flops=flops, bytes_accessed=blk.size * 2 + 2 * levels * rows * cols * chans * 2, transcendentals=0
        ),
    )(blk, both)


def local(field, weights, coefs, land_mask, fold_flag):
    layers, taps = weights.shape[0], weights.shape[1]
    levels, rows, channels, cols = field.shape
    fold_sign = jnp.where(fold_flag == 1, -1.0, 1.0).astype(jnp.bfloat16)
    coef_stack = (
        coefs.reshape(layers, levels, rows, taps, cols)
        .transpose(1, 2, 0, 3, 4)
        .reshape(levels, rows, layers * taps, cols)
    )
    mask_stack = land_mask.astype(jnp.bfloat16)[:, :, None, :]
    block_in = jnp.concatenate([field, coef_stack, mask_stack], axis=2)
    block = block_in.transpose(0, 1, 3, 2)
    ext = exchange(block, block_in, fold_sign, taps, layers, channels)

    is_top = lax.axis_index("lat") == lax.axis_size("lat") - 1
    flipped = weights[:, ::-1] * fold_sign[None, None, :, None] * fold_sign[None, None, None, :]
    weights_high = jnp.where(is_top, flipped, weights)
    both = jnp.stack([weights, weights_high], axis=1)

    return run_model(ext, both, rows, cols, layers, taps, HALO + rows)


def solution(mesh):
    return jax.shard_map(
        local,
        mesh=mesh,
        in_specs=(
            P(None, "lat", None, "lon"),
            P(),
            P(None, "lat", None, "lon"),
            P(None, "lat", "lon"),
            P(),
        ),
        out_specs=(P(None, "lat", None, "lon"), P(None, "lat", None, "lon")),
        check_vma=False,
    )
```

profile of v0, /device:TPU:31, one launch (start us, length us, event | category | flops | bytes accessed | tf_op | source)
XLA Modules:
  0.0 84.7 jit_solution(9510787198957998407)
XLA Ops:
  0.6 0.9 %copy.14 = bf16[2,8,2,9,128]{4,1,3,2,0:T(8,128)(2,1)S(1)} copy(bf16[2,8,2,9,128]{4,1,3,0,2:T(8,128)(2,1)} %bitcast.19) | data formatting | bytes 147456 | tf_op jit(solution)/shard_map/transpose | solution.py:165
  1.5 0.3 copy.16
  1.8 0.7 convert_bitcast_fusion
  2.5 0.3 copy.17
  2.9 1.3 %copy.15 = bf16[2,8,128,128]{2,3,1,0:T(8,128)(2,1)S(1)} copy(bf16[2,8,128,128]{3,2,1,0:T(8,128)(2,1)} %param.5) | data formatting | bytes 1048576 | tf_op args[0]
  4.2 0.3 fusion.4
  4.5 0.0 copy-start.6
  4.5 0.0 copy-start
  4.6 3.9 %collective-permute-start = (bf16[2,8,4,147]{3,2,1,0:T(4,128)(2,1)S(1)}, bf16[2,8,4,147]{3,2,1,0:T(4,128)(2,1)S(1)}, u32[]{:S(2)}, u32[]{:S(2)}) collective-permute-start(bf16[2,8,4,147]{3,2,1,0:T(4,128)(2,1)S(1)} %get-tuple-element.6), channel_id=1, source_target_pairs={{0,16},{16,32},{32,48},{48,64},{64,80},{80,96},{96,112},{112,128},... | collective-permute-start | bytes 56456 | tf_op jit(solution)/shard_map/ppermute | solution.py:21
  8.4 1.9 %collective-permute-start.1 = (bf16[2,8,4,147]{3,2,1,0:T(4,128)(2,1)S(1)}, bf16[2,8,4,147]{3,2,1,0:T(4,128)(2,1)S(1)}, u32[]{:S(2)}, u32[]{:S(2)}) collective-permute-start(bf16[2,8,4,147]{3,2,1,0:T(4,128)(2,1)S(1)} %get-tuple-element.7), channel_id=1, source_target_pairs={{16,0},{32,16},{48,32},{64,48},{80,64},{96,80},{112,96},{128,112},... | collective-permute-start | bytes 56456 | tf_op jit(solution)/shard_map/ppermute | solution.py:22
  10.4 0.6 fusion.2
  11.0 11.2 %collective-permute-start.3 = (bf16[2,4,4,147]{3,2,1,0:T(4,128)(2,1)}, bf16[2,4,4,147]{3,2,1,0:T(4,128)(2,1)}, u32[]{:S(2)}, u32[]{:S(2)}) collective-permute-start(bf16[2,4,4,147]{3,2,1,0:T(4,128)(2,1)} %get-tuple-element.4), channel_id=1, source_target_pairs={{15,495},{31,479},{47,463},{63,447},{79,431},{95,415},{111,399},{1... | collective-permute-start | bytes 28232 | tf_op jit(solution)/shard_map/ppermute | solution.py:29
  22.2 1.9 %collective-permute-start.5 = (bf16[2,4,4,147]{3,2,1,0:T(4,128)(2,1)}, bf16[2,4,4,147]{3,2,1,0:T(4,128)(2,1)}, u32[]{:S(2)}, u32[]{:S(2)}) collective-permute-start(bf16[2,4,4,147]{3,2,1,0:T(4,128)(2,1)} %get-tuple-element.5), channel_id=1, source_target_pairs={{15,15},{31,511},{47,495},{63,479},{79,463},{95,447},{111,431},{12... | collective-permute-start | bytes 28232 | tf_op jit(solution)/shard_map/ppermute | solution.py:29
  24.1 0.3 pad_maximum_fusion.3
  24.5 0.8 slice.59
  25.3 6.5 %collective-permute-start.4 = (bf16[2,4,147,128]{2,3,1,0:T(8,128)(2,1)}, bf16[2,4,147,128]{2,3,1,0:T(8,128)(2,1)S(1)}, u32[]{:S(2)}, u32[]{:S(2)}) collective-permute-start(bf16[2,4,147,128]{2,3,1,0:T(8,128)(2,1)} %slice.59), channel_id=1, source_target_pairs={{15,511},{31,495},{47,479},{63,463},{79,447},{95,431},{111,415},{1... | collective-permute-start | bytes 903176 | tf_op jit(solution)/shard_map/ppermute | solution.py:29
  31.9 0.0 copy-done.6
  31.9 0.0 copy-start.5
  31.9 0.0 copy-done
  31.9 0.3 select_bitcast_fusion
  32.2 1.1 %pad_maximum_fusion.1.w_ref = bf16[2,2,9,128,128]{4,3,2,1,0:T(8,128)(2,1)} fusion(bf16[2,1,9,128,128]{4,3,2,1,0:T(8,128)(2,1)S(1)} %select_bitcast_fusion, bf16[2,1,9,128,128]{4,3,2,1,0:T(8,128)(2,1)S(1)} %bitcast.14), kind=kLoop, calls=%fused_computation.1 | loop fusion | flops 589824 | bytes 2359296 | tf_op jit(solution)/shard_map/stack | solution.py:176
  33.3 0.0 collective-permute-done
  33.3 0.0 copy-start.1
  33.3 0.0 collective-permute-done.1
  33.3 0.6 copy-done.1
  34.0 0.0 copy-start.3
  34.0 0.6 copy-done.3
  34.6 0.5 pad_maximum_fusion.2
  35.1 0.9 %fusion.1 = (bf16[2,4,136,147]{3,2,1,0:T(8,128)(2,1)S(1)}, bf16[2,4,136,147]{3,2,1,0:T(8,128)(2,1)}) fusion(bf16[2,8,136,147]{3,2,1,0:T(8,128)(2,1)S(1)} %pad_maximum_fusion.2), kind=kLoop, calls=%fused_computation.11 | loop fusion | bytes 1279488 | tf_op jit(solution)/shard_map/slice | solution.py:39
  36.0 2.1 %collective-permute-start.6 = (bf16[2,4,136,147]{3,2,1,0:T(8,128)(2,1)}, bf16[2,4,136,147]{3,2,1,0:T(8,128)(2,1)}, u32[]{:S(2)}, u32[]{:S(2)}) collective-permute-start(bf16[2,4,136,147]{3,2,1,0:T(8,128)(2,1)} %get-tuple-element.3), channel_id=1, source_target_pairs={{1,0},{2,1},{3,2},{4,3},{5,4},{6,5},{7,6},{8,7},{9,8},{10,9},{11,1... | collective-permute-start | bytes 959624 | tf_op jit(solution)/shard_map/ppermute | solution.py:40
  38.1 1.5 %collective-permute-start.2 = (bf16[2,4,136,147]{3,2,1,0:T(8,128)(2,1)S(1)}, bf16[2,4,136,147]{3,2,1,0:T(8,128)(2,1)S(1)}, u32[]{:S(2)}, u32[]{:S(2)}) collective-permute-start(bf16[2,4,136,147]{3,2,1,0:T(8,128)(2,1)S(1)} %get-tuple-element.2), channel_id=1, source_target_pairs={{0,1},{1,2},{2,3},{3,4},{4,5},{5,6},{6,7},{7,8},{8,9},{9,10},{10,1... | collective-permute-start | bytes 959624 | tf_op jit(solution)/shard_map/ppermute | solution.py:39
  39.5 0.0 collective-permute-done.3
  39.5 0.0 collective-permute-done.5
  39.6 16.3 %collective-permute-done.4 = bf16[2,4,147,128]{2,3,1,0:T(8,128)(2,1)S(1)} collective-permute-done((bf16[2,4,147,128]{2,3,1,0:T(8,128)(2,1)}, bf16[2,4,147,128]{2,3,1,0:T(8,128)(2,1)S(1)}, u32[]{:S(2)}, u32[]{:S(2)}) %collective-permute-start.4) | collective-permute-done | bytes 301088 | tf_op jit(solution)/shard_map/ppermute | solution.py:29
  55.8 0.9 %pad_maximum_fusion.4 = bf16[2,4,136,147]{3,2,1,0:T(8,128)(2,1)S(1)} fusion(bf16[2,4,4,147]{3,2,1,0:T(4,128)(2,1)} %collective-permute-done.5, bf16[2,4,128,147]{3,2,1,0:T(8,128)(2,1)S(1)} %bitcast.15, bf16[2,4,4,147]{3,2,1,0:T(4,128)(2,1)} %collective-permute-done.3), kind=kLoop, calls=%fused_computation.5 | loop fusion | flops 959616 | bytes 639744 | tf_op jit(solution)/shard_map/concatenate | solution.py:34
  56.8 0.0 copy-done.5
  56.8 1.0 %slice.49 = bf16[2,4,136,128]{3,2,1,0:T(8,128)(2,1)S(1)} reverse(bf16[2,4,136,128]{3,2,1,0:T(8,128)(2,1)S(1)} %slice.61), dimensions={1,2} | reverse | bytes 557056 | tf_op jit(solution)/shard_map/slice | solution.py:42
  57.8 0.7 broadcast_multiply_fusion
  58.5 0.1 slice.63
  58.7 0.0 copy-start.2
  58.7 0.0 copy-start.4
  58.7 1.0 %slice.51 = bf16[2,4,136,18]{3,2,1,0:T(8,128)(2,1)S(1)} reverse(bf16[2,4,136,18]{3,2,1,0:T(8,128)(2,1)S(1)} %slice.62), dimensions={1,2} | reverse | bytes 78336 | tf_op jit(solution)/shard_map/slice | solution.py:43
  59.7 0.2 copy.18
  60.0 0.3 copy.19
  60.3 1.0 %slice.53 = bf16[2,4,136,1]{3,2,1,0:T(8,128)(2,1)S(1)} reverse(bf16[2,4,136,1]{3,2,1,0:T(8,128)(2,1)S(1)} %slice.63), dimensions={1,2} | reverse | bytes 4352 | tf_op jit(solution)/shard_map/slice | solution.py:47
  61.3 0.0 collective-permute-done.6
  61.3 0.3 maximum_select_fusion
  61.5 0.0 collective-permute-done.2
  61.5 0.0 copy-done.2
  61.6 0.0 copy-done.4
  61.6 1.8 %pad_maximum_fusion.blk_ref = bf16[2,16,136,147]{3,2,1,0:T(8,128)(2,1)} fusion(bf16[2,4,136,147]{3,2,1,0:T(8,128)(2,1)S(1)} %maximum_select_fusion, bf16[2,8,4,147]{3,2,1,0:T(4,128)(2,1)S(1)} %copy-done.4, bf16[2,8,128,147]{3,2,1,0:T(8,128)(2,1)S(1)} %fusion.4, bf16[2,8,4,147]{3,2,1,0:T(4,128)(2,1)S(1)} %copy-done.2, ...), kind=kLoop, calls=%fused_computation | loop fusion | flops 6397440 | bytes 2558976 | tf_op jit(solution)/shard_map/concatenate | solution.py:51
  63.3 21.3 %shard_map.68 = (bf16[2,8,128,128]{3,2,1,0:T(8,128)(2,1)}, bf16[2,8,128,128]{3,2,1,0:T(8,128)(2,1)}) custom-call(bf16[2,16,136,147]{3,2,1,0:T(8,128)(2,1)} %pad_maximum_fusion.blk_ref, bf16[2,2,9,128,128]{4,3,2,1,0:T(8,128)(2,1)} %pad_maximum_fusion.1.w_ref), custom_call_target="tpu_custom_call" | custom-call | flops 3529506816 | bytes 2328064 | tf_op jit(solution)/shard_map/pallas_call | solution.py:139
  (5 shorter events, 0.2 us)
Async XLA Ops:
  4.5 27.3 %copy-start.6 = (s32[128]{0:T(128)S(1)}, s32[128]{0:T(128)}, u32[]{:S(2)}) copy-start(s32[128]{0:T(128)} %param.9) | copy-start | bytes 1540
  4.5 27.4 %copy-start = (bf16[2,9,128,128]{3,2,1,0:T(8,128)(2,1)S(1)}, bf16[2,9,128,128]{3,2,1,0:T(8,128)(2,1)}, u32[]{:S(2)}) copy-start(bf16[2,9,128,128]{3,2,1,0:T(8,128)(2,1)} %param.6) | copy-start | bytes 1769476
  4.6 28.8 %collective-permute-start = (bf16[2,8,4,147]{3,2,1,0:T(4,128)(2,1)S(1)}, bf16[2,8,4,147]{3,2,1,0:T(4,128)(2,1)S(1)}, u32[]{:S(2)}, u32[]{:S(2)}) collective-permute-start(bf16[2,8,4,147]{3,2,1,0:T(4,128)(2,1)S(1)} %get-tuple-element.6), channel_id=1, source_target_pairs={{0,16},{16,32},{32,48},{48,64},{64,80},{80,96},{96,112},{112,128},... | collective-permute-start | bytes 56456 | tf_op jit(solution)/shard_map/ppermute | solution.py:21
  8.4 24.9 %collective-permute-start.1 = (bf16[2,8,4,147]{3,2,1,0:T(4,128)(2,1)S(1)}, bf16[2,8,4,147]{3,2,1,0:T(4,128)(2,1)S(1)}, u32[]{:S(2)}, u32[]{:S(2)}) collective-permute-start(bf16[2,8,4,147]{3,2,1,0:T(4,128)(2,1)S(1)} %get-tuple-element.7), channel_id=1, source_target_pairs={{16,0},{32,16},{48,32},{64,48},{80,64},{96,80},{112,96},{128,112},... | collective-permute-start | bytes 56456 | tf_op jit(solution)/shard_map/ppermute | solution.py:22
  11.0 28.5 %collective-permute-start.3 = (bf16[2,4,4,147]{3,2,1,0:T(4,128)(2,1)}, bf16[2,4,4,147]{3,2,1,0:T(4,128)(2,1)}, u32[]{:S(2)}, u32[]{:S(2)}) collective-permute-start(bf16[2,4,4,147]{3,2,1,0:T(4,128)(2,1)} %get-tuple-element.4), channel_id=1, source_target_pairs={{15,495},{31,479},{47,463},{63,447},{79,431},{95,415},{111,399},{1... | collective-permute-start | bytes 28232 | tf_op jit(solution)/shard_map/ppermute | solution.py:29
  22.2 17.4 %collective-permute-start.5 = (bf16[2,4,4,147]{3,2,1,0:T(4,128)(2,1)}, bf16[2,4,4,147]{3,2,1,0:T(4,128)(2,1)}, u32[]{:S(2)}, u32[]{:S(2)}) collective-permute-start(bf16[2,4,4,147]{3,2,1,0:T(4,128)(2,1)} %get-tuple-element.5), channel_id=1, source_target_pairs={{15,15},{31,511},{47,495},{63,479},{79,463},{95,447},{111,431},{12... | collective-permute-start | bytes 28232 | tf_op jit(solution)/shard_map/ppermute | solution.py:29
  25.3 30.5 %collective-permute-start.4 = (bf16[2,4,147,128]{2,3,1,0:T(8,128)(2,1)}, bf16[2,4,147,128]{2,3,1,0:T(8,128)(2,1)S(1)}, u32[]{:S(2)}, u32[]{:S(2)}) collective-permute-start(bf16[2,4,147,128]{2,3,1,0:T(8,128)(2,1)} %slice.59), channel_id=1, source_target_pairs={{15,511},{31,495},{47,479},{63,463},{79,447},{95,431},{111,415},{1... | collective-permute-start | bytes 903176 | tf_op jit(solution)/shard_map/ppermute | solution.py:29
  31.9 24.9 %copy-start.5 = (bf16[128]{0:T(256)(128)(2,1)}, bf16[128]{0:T(256)(128)(2,1)S(1)}, u32[]{:S(2)}) copy-start(bf16[128]{0:T(256)(128)(2,1)S(1)} %fusion) | copy-start | bytes 772
  33.3 0.6 copy-start.1
  34.0 0.6 copy-start.3
  36.0 25.3 %collective-permute-start.6 = (bf16[2,4,136,147]{3,2,1,0:T(8,128)(2,1)}, bf16[2,4,136,147]{3,2,1,0:T(8,128)(2,1)}, u32[]{:S(2)}, u32[]{:S(2)}) collective-permute-start(bf16[2,4,136,147]{3,2,1,0:T(8,128)(2,1)} %get-tuple-element.3), channel_id=1, source_target_pairs={{1,0},{2,1},{3,2},{4,3},{5,4},{6,5},{7,6},{8,7},{9,8},{10,9},{11,1... | collective-permute-start | bytes 959624 | tf_op jit(solution)/shard_map/ppermute | solution.py:40
  38.1 23.5 %collective-permute-start.2 = (bf16[2,4,136,147]{3,2,1,0:T(8,128)(2,1)S(1)}, bf16[2,4,136,147]{3,2,1,0:T(8,128)(2,1)S(1)}, u32[]{:S(2)}, u32[]{:S(2)}) collective-permute-start(bf16[2,4,136,147]{3,2,1,0:T(8,128)(2,1)S(1)} %get-tuple-element.2), channel_id=1, source_target_pairs={{0,1},{1,2},{2,3},{3,4},{4,5},{5,6},{6,7},{7,8},{8,9},{9,10},{10,1... | collective-permute-start | bytes 959624 | tf_op jit(solution)/shard_map/ppermute | solution.py:39
  58.7 2.9 %copy-start.2 = (bf16[2,8,4,147]{3,2,1,0:T(4,128)(2,1)S(1)}, bf16[2,8,4,147]{3,2,1,0:T(4,128)(2,1)}, u32[]{:S(2)}) copy-start(bf16[2,8,4,147]{3,2,1,0:T(4,128)(2,1)} %copy-done.1) | copy-start | bytes 56452
  58.7 2.9 %copy-start.4 = (bf16[2,8,4,147]{3,2,1,0:T(4,128)(2,1)S(1)}, bf16[2,8,4,147]{3,2,1,0:T(4,128)(2,1)}, u32[]{:S(2)}) copy-start(bf16[2,8,4,147]{3,2,1,0:T(4,128)(2,1)} %copy-done.3) | copy-start | bytes 56452
where the time goes:
time: 85.2 us; the launch traced here: 84.7 us
  starting transfers between devices  29 us (34%)
  Pallas kernels  21.3 us (25%)
  waiting for transfers between devices  16.3 us (19%)
  local copies, waits for them, and re-layouts  10.2 us (12%)
  other arithmetic  6.91 us (8%)
  between operations  0.93 us (1%)
    pallas_call x1, Pallas kernels, run_model(): pl.pallas_call(kernel, out_shape=(out, out), in_specs=[pl.BlockSpec(memor...  21.3 us
    ppermute x3, starting transfers between devices, across(): return lax.ppermute(piece, ('lon', 'lat'), pairs)  19.7 us
    ppermute x3, waiting for transfers between devices, across(): return lax.ppermute(piece, ('lon', 'lat'), pairs)  16.3 us
    ppermute x1, starting transfers between devices, exchange(): from_left = lax.ppermute(block[:, :, cols - HALO:], 'lon', to_right)  3.86 us
    unnamed x15, local copies, waits for them, and re-layouts  2.57 us
    ppermute x1, starting transfers between devices, exchange(): above = lax.ppermute(wide[:, :HALO], 'lat', to_down)  2.1 us
    ppermute x1, starting transfers between devices, exchange(): from_right = lax.ppermute(block[:, :, :HALO], 'lon', to_left)  1.92 us
    concatenate x1, other arithmetic, exchange(): return jnp.concatenate([below, wide, above], axis=1)  1.76 us
  transfers between devices with their start and end apart: 7, of which 1 were waited for; matrix products, arithmetic and copies ran while one was open for 12% of the time, Pallas kernels for 0%

commit v1 on v0

--- a/solution.py
+++ b/solution.py
@@ -100,7 +100,9 @@
     data_cols = blk_ref.shape[2]
     mask_lane = layers * taps
     for buf in (ext_ref, aux_ref, x1_ref, x2_ref, g1_ref):
-        buf[...] = jnp.zeros(buf.shape, buf.dtype)
+        edge = buf.shape[:2] + (PAD, buf.shape[3])
+        buf[:, :, pl.ds(0, PAD), :] = jnp.zeros(edge, buf.dtype)
+        buf[:, :, pl.ds(buf.shape[2] - PAD, PAD), :] = jnp.zeros(edge, buf.dtype)
     for lev in range(levels):
         for j in range(total_rows):
             piece = blk_ref[lev, j].astype(jnp.float32)

time: 85.2 us -> 84.7 us (level)
  no operation moved by 1% of the time
where the time goes in v1:
time: 84.7 us; the launch traced here: 84.1 us
  starting transfers between devices  29 us (34%)
  Pallas kernels  20.8 us (25%)
  waiting for transfers between devices  16.3 us (19%)
  local copies, waits for them, and re-layouts  10.2 us (12%)
  other arithmetic  6.91 us (8%)
  between operations  0.93 us (1%)
    pallas_call x1, Pallas kernels, run_model(): pl.pallas_call(kernel, out_shape=(out, out), in_specs=[pl.BlockSpec(memor...  20.8 us
    ppermute x3, starting transfers between devices, across(): return lax.ppermute(piece, ('lon', 'lat'), pairs)  19.7 us
    ppermute x3, waiting for transfers between devices, across(): return lax.ppermute(piece, ('lon', 'lat'), pairs)  16.3 us
    ppermute x1, starting transfers between devices, exchange(): from_left = lax.ppermute(block[:, :, cols - HALO:], 'lon', to_right)  3.86 us
    unnamed x15, local copies, waits for them, and re-layouts  2.57 us
    ppermute x1, starting transfers between devices, exchange(): above = lax.ppermute(wide[:, :HALO], 'lat', to_down)  2.1 us
    ppermute x1, starting transfers between devices, exchange(): from_right = lax.ppermute(block[:, :, :HALO], 'lon', to_left)  1.92 us
    concatenate x1, other arithmetic, exchange(): return jnp.concatenate([below, wide, above], axis=1)  1.76 us
  transfers between devices with their start and end apart: 7, of which 1 were waited for; matrix products, arithmetic and copies ran while one was open for 12% of the time, Pallas kernels for 0%

profile of v1, /device:TPU:31, one launch (start us, length us, event | category | flops | bytes accessed | tf_op | source)
XLA Modules:
  0.0 84.1 jit_solution(10473696405599651986)
XLA Ops:
  0.6 0.9 %copy.14 = bf16[2,8,2,9,128]{4,1,3,2,0:T(8,128)(2,1)S(1)} copy(bf16[2,8,2,9,128]{4,1,3,0,2:T(8,128)(2,1)} %bitcast.19) | data formatting | bytes 147456 | tf_op jit(solution)/shard_map/transpose | solution.py:167
  1.5 0.3 copy.16
  1.8 0.7 convert_bitcast_fusion
  2.5 0.3 copy.17
  2.9 1.3 %copy.15 = bf16[2,8,128,128]{2,3,1,0:T(8,128)(2,1)S(1)} copy(bf16[2,8,128,128]{3,2,1,0:T(8,128)(2,1)} %param.5) | data formatting | bytes 1048576 | tf_op args[0]
  4.2 0.3 fusion.4
  4.5 0.0 copy-start.6
  4.5 0.0 copy-start
  4.6 3.9 %collective-permute-start = (bf16[2,8,4,147]{3,2,1,0:T(4,128)(2,1)S(1)}, bf16[2,8,4,147]{3,2,1,0:T(4,128)(2,1)S(1)}, u32[]{:S(2)}, u32[]{:S(2)}) collective-permute-start(bf16[2,8,4,147]{3,2,1,0:T(4,128)(2,1)S(1)} %get-tuple-element.6), channel_id=1, source_target_pairs={{0,16},{16,32},{32,48},{48,64},{64,80},{80,96},{96,112},{112,128},... | collective-permute-start | bytes 56456 | tf_op jit(solution)/shard_map/ppermute | solution.py:21
  8.4 1.9 %collective-permute-start.1 = (bf16[2,8,4,147]{3,2,1,0:T(4,128)(2,1)S(1)}, bf16[2,8,4,147]{3,2,1,0:T(4,128)(2,1)S(1)}, u32[]{:S(2)}, u32[]{:S(2)}) collective-permute-start(bf16[2,8,4,147]{3,2,1,0:T(4,128)(2,1)S(1)} %get-tuple-element.7), channel_id=1, source_target_pairs={{16,0},{32,16},{48,32},{64,48},{80,64},{96,80},{112,96},{128,112},... | collective-permute-start | bytes 56456 | tf_op jit(solution)/shard_map/ppermute | solution.py:22
  10.4 0.6 fusion.2
  11.0 11.2 %collective-permute-start.3 = (bf16[2,4,4,147]{3,2,1,0:T(4,128)(2,1)}, bf16[2,4,4,147]{3,2,1,0:T(4,128)(2,1)}, u32[]{:S(2)}, u32[]{:S(2)}) collective-permute-start(bf16[2,4,4,147]{3,2,1,0:T(4,128)(2,1)} %get-tuple-element.4), channel_id=1, source_target_pairs={{15,495},{31,479},{47,463},{63,447},{79,431},{95,415},{111,399},{1... | collective-permute-start | bytes 28232 | tf_op jit(solution)/shard_map/ppermute | solution.py:29
  22.2 1.9 %collective-permute-start.5 = (bf16[2,4,4,147]{3,2,1,0:T(4,128)(2,1)}, bf16[2,4,4,147]{3,2,1,0:T(4,128)(2,1)}, u32[]{:S(2)}, u32[]{:S(2)}) collective-permute-start(bf16[2,4,4,147]{3,2,1,0:T(4,128)(2,1)} %get-tuple-element.5), channel_id=1, source_target_pairs={{15,15},{31,511},{47,495},{63,479},{79,463},{95,447},{111,431},{12... | collective-permute-start | bytes 28232 | tf_op jit(solution)/shard_map/ppermute | solution.py:29
  24.1 0.3 pad_maximum_fusion.3
  24.5 0.8 slice.59
  25.3 6.5 %collective-permute-start.4 = (bf16[2,4,147,128]{2,3,1,0:T(8,128)(2,1)}, bf16[2,4,147,128]{2,3,1,0:T(8,128)(2,1)S(1)}, u32[]{:S(2)}, u32[]{:S(2)}) collective-permute-start(bf16[2,4,147,128]{2,3,1,0:T(8,128)(2,1)} %slice.59), channel_id=1, source_target_pairs={{15,511},{31,495},{47,479},{63,463},{79,447},{95,431},{111,415},{1... | collective-permute-start | bytes 903176 | tf_op jit(solution)/shard_map/ppermute | solution.py:29
  31.9 0.0 copy-done.6
  31.9 0.0 copy-start.5
  31.9 0.0 copy-done
  31.9 0.3 select_bitcast_fusion
  32.2 1.1 %pad_maximum_fusion.1.w_ref = bf16[2,2,9,128,128]{4,3,2,1,0:T(8,128)(2,1)} fusion(bf16[2,1,9,128,128]{4,3,2,1,0:T(8,128)(2,1)S(1)} %select_bitcast_fusion, bf16[2,1,9,128,128]{4,3,2,1,0:T(8,128)(2,1)S(1)} %bitcast.14), kind=kLoop, calls=%fused_computation.1 | loop fusion | flops 589824 | bytes 2359296 | tf_op jit(solution)/shard_map/stack | solution.py:178
  33.3 0.0 collective-permute-done
  33.3 0.0 copy-start.1
  33.3 0.0 collective-permute-done.1
  33.3 0.6 copy-done.1
  34.0 0.0 copy-start.3
  34.0 0.6 copy-done.3
  34.6 0.5 pad_maximum_fusion.2
  35.1 0.9 %fusion.1 = (bf16[2,4,136,147]{3,2,1,0:T(8,128)(2,1)S(1)}, bf16[2,4,136,147]{3,2,1,0:T(8,128)(2,1)}) fusion(bf16[2,8,136,147]{3,2,1,0:T(8,128)(2,1)S(1)} %pad_maximum_fusion.2), kind=kLoop, calls=%fused_computation.11 | loop fusion | bytes 1279488 | tf_op jit(solution)/shard_map/slice | solution.py:39
  36.0 2.1 %collective-permute-start.6 = (bf16[2,4,136,147]{3,2,1,0:T(8,128)(2,1)}, bf16[2,4,136,147]{3,2,1,0:T(8,128)(2,1)}, u32[]{:S(2)}, u32[]{:S(2)}) collective-permute-start(bf16[2,4,136,147]{3,2,1,0:T(8,128)(2,1)} %get-tuple-element.3), channel_id=1, source_target_pairs={{1,0},{2,1},{3,2},{4,3},{5,4},{6,5},{7,6},{8,7},{9,8},{10,9},{11,1... | collective-permute-start | bytes 959624 | tf_op jit(solution)/shard_map/ppermute | solution.py:40
  38.1 1.5 %collective-permute-start.2 = (bf16[2,4,136,147]{3,2,1,0:T(8,128)(2,1)S(1)}, bf16[2,4,136,147]{3,2,1,0:T(8,128)(2,1)S(1)}, u32[]{:S(2)}, u32[]{:S(2)}) collective-permute-start(bf16[2,4,136,147]{3,2,1,0:T(8,128)(2,1)S(1)} %get-tuple-element.2), channel_id=1, source_target_pairs={{0,1},{1,2},{2,3},{3,4},{4,5},{5,6},{6,7},{7,8},{8,9},{9,10},{10,1... | collective-permute-start | bytes 959624 | tf_op jit(solution)/shard_map/ppermute | solution.py:39
  39.5 0.0 collective-permute-done.3
  39.5 0.0 collective-permute-done.5
  39.6 16.3 %collective-permute-done.4 = bf16[2,4,147,128]{2,3,1,0:T(8,128)(2,1)S(1)} collective-permute-done((bf16[2,4,147,128]{2,3,1,0:T(8,128)(2,1)}, bf16[2,4,147,128]{2,3,1,0:T(8,128)(2,1)S(1)}, u32[]{:S(2)}, u32[]{:S(2)}) %collective-permute-start.4) | collective-permute-done | bytes 301088 | tf_op jit(solution)/shard_map/ppermute | solution.py:29
  55.8 0.9 %pad_maximum_fusion.4 = bf16[2,4,136,147]{3,2,1,0:T(8,128)(2,1)S(1)} fusion(bf16[2,4,4,147]{3,2,1,0:T(4,128)(2,1)} %collective-permute-done.5, bf16[2,4,128,147]{3,2,1,0:T(8,128)(2,1)S(1)} %bitcast.15, bf16[2,4,4,147]{3,2,1,0:T(4,128)(2,1)} %collective-permute-done.3), kind=kLoop, calls=%fused_computation.5 | loop fusion | flops 959616 | bytes 639744 | tf_op jit(solution)/shard_map/concatenate | solution.py:34
  56.8 0.0 copy-done.5
  56.8 1.0 %slice.49 = bf16[2,4,136,128]{3,2,1,0:T(8,128)(2,1)S(1)} reverse(bf16[2,4,136,128]{3,2,1,0:T(8,128)(2,1)S(1)} %slice.61), dimensions={1,2} | reverse | bytes 557056 | tf_op jit(solution)/shard_map/slice | solution.py:42
  57.8 0.7 broadcast_multiply_fusion
  58.5 0.1 slice.63
  58.7 0.0 copy-start.2
  58.7 0.0 copy-start.4
  58.7 1.0 %slice.51 = bf16[2,4,136,18]{3,2,1,0:T(8,128)(2,1)S(1)} reverse(bf16[2,4,136,18]{3,2,1,0:T(8,128)(2,1)S(1)} %slice.62), dimensions={1,2} | reverse | bytes 78336 | tf_op jit(solution)/shard_map/slice | solution.py:43
  59.7 0.2 copy.18
  60.0 0.3 copy.19
  60.3 1.0 %slice.53 = bf16[2,4,136,1]{3,2,1,0:T(8,128)(2,1)S(1)} reverse(bf16[2,4,136,1]{3,2,1,0:T(8,128)(2,1)S(1)} %slice.63), dimensions={1,2} | reverse | bytes 4352 | tf_op jit(solution)/shard_map/slice | solution.py:47
  61.3 0.0 collective-permute-done.6
  61.3 0.3 maximum_select_fusion
  61.5 0.0 collective-permute-done.2
  61.5 0.0 copy-done.2
  61.6 0.0 copy-done.4
  61.6 1.8 %pad_maximum_fusion.blk_ref = bf16[2,16,136,147]{3,2,1,0:T(8,128)(2,1)} fusion(bf16[2,4,136,147]{3,2,1,0:T(8,128)(2,1)S(1)} %maximum_select_fusion, bf16[2,8,4,147]{3,2,1,0:T(4,128)(2,1)S(1)} %copy-done.4, bf16[2,8,128,147]{3,2,1,0:T(8,128)(2,1)S(1)} %fusion.4, bf16[2,8,4,147]{3,2,1,0:T(4,128)(2,1)S(1)} %copy-done.2, ...), kind=kLoop, calls=%fused_computation | loop fusion | flops 6397440 | bytes 2558976 | tf_op jit(solution)/shard_map/concatenate | solution.py:51
  63.3 20.8 %shard_map.68 = (bf16[2,8,128,128]{3,2,1,0:T(8,128)(2,1)}, bf16[2,8,128,128]{3,2,1,0:T(8,128)(2,1)}) custom-call(bf16[2,16,136,147]{3,2,1,0:T(8,128)(2,1)} %pad_maximum_fusion.blk_ref, bf16[2,2,9,128,128]{4,3,2,1,0:T(8,128)(2,1)} %pad_maximum_fusion.1.w_ref), custom_call_target="tpu_custom_call" | custom-call | flops 3529506816 | bytes 2328064 | tf_op jit(solution)/shard_map/pallas_call | solution.py:141
  (5 shorter events, 0.2 us)
Async XLA Ops:
  4.5 27.3 %copy-start.6 = (s32[128]{0:T(128)S(1)}, s32[128]{0:T(128)}, u32[]{:S(2)}) copy-start(s32[128]{0:T(128)} %param.9) | copy-start | bytes 1540
  4.5 27.4 %copy-start = (bf16[2,9,128,128]{3,2,1,0:T(8,128)(2,1)S(1)}, bf16[2,9,128,128]{3,2,1,0:T(8,128)(2,1)}, u32[]{:S(2)}) copy-start(bf16[2,9,128,128]{3,2,1,0:T(8,128)(2,1)} %param.6) | copy-start | bytes 1769476
  4.6 28.8 %collective-permute-start = (bf16[2,8,4,147]{3,2,1,0:T(4,128)(2,1)S(1)}, bf16[2,8,4,147]{3,2,1,0:T(4,128)(2,1)S(1)}, u32[]{:S(2)}, u32[]{:S(2)}) collective-permute-start(bf16[2,8,4,147]{3,2,1,0:T(4,128)(2,1)S(1)} %get-tuple-element.6), channel_id=1, source_target_pairs={{0,16},{16,32},{32,48},{48,64},{64,80},{80,96},{96,112},{112,128},... | collective-permute-start | bytes 56456 | tf_op jit(solution)/shard_map/ppermute | solution.py:21
  8.4 24.9 %collective-permute-start.1 = (bf16[2,8,4,147]{3,2,1,0:T(4,128)(2,1)S(1)}, bf16[2,8,4,147]{3,2,1,0:T(4,128)(2,1)S(1)}, u32[]{:S(2)}, u32[]{:S(2)}) collective-permute-start(bf16[2,8,4,147]{3,2,1,0:T(4,128)(2,1)S(1)} %get-tuple-element.7), channel_id=1, source_target_pairs={{16,0},{32,16},{48,32},{64,48},{80,64},{96,80},{112,96},{128,112},... | collective-permute-start | bytes 56456 | tf_op jit(solution)/shard_map/ppermute | solution.py:22
  11.0 28.5 %collective-permute-start.3 = (bf16[2,4,4,147]{3,2,1,0:T(4,128)(2,1)}, bf16[2,4,4,147]{3,2,1,0:T(4,128)(2,1)}, u32[]{:S(2)}, u32[]{:S(2)}) collective-permute-start(bf16[2,4,4,147]{3,2,1,0:T(4,128)(2,1)} %get-tuple-element.4), channel_id=1, source_target_pairs={{15,495},{31,479},{47,463},{63,447},{79,431},{95,415},{111,399},{1... | collective-permute-start | bytes 28232 | tf_op jit(solution)/shard_map/ppermute | solution.py:29
  22.2 17.4 %collective-permute-start.5 = (bf16[2,4,4,147]{3,2,1,0:T(4,128)(2,1)}, bf16[2,4,4,147]{3,2,1,0:T(4,128)(2,1)}, u32[]{:S(2)}, u32[]{:S(2)}) collective-permute-start(bf16[2,4,4,147]{3,2,1,0:T(4,128)(2,1)} %get-tuple-element.5), channel_id=1, source_target_pairs={{15,15},{31,511},{47,495},{63,479},{79,463},{95,447},{111,431},{12... | collective-permute-start | bytes 28232 | tf_op jit(solution)/shard_map/ppermute | solution.py:29
  25.3 30.5 %collective-permute-start.4 = (bf16[2,4,147,128]{2,3,1,0:T(8,128)(2,1)}, bf16[2,4,147,128]{2,3,1,0:T(8,128)(2,1)S(1)}, u32[]{:S(2)}, u32[]{:S(2)}) collective-permute-start(bf16[2,4,147,128]{2,3,1,0:T(8,128)(2,1)} %slice.59), channel_id=1, source_target_pairs={{15,511},{31,495},{47,479},{63,463},{79,447},{95,431},{111,415},{1... | collective-permute-start | bytes 903176 | tf_op jit(solution)/shard_map/ppermute | solution.py:29
  31.9 24.9 %copy-start.5 = (bf16[128]{0:T(256)(128)(2,1)}, bf16[128]{0:T(256)(128)(2,1)S(1)}, u32[]{:S(2)}) copy-start(bf16[128]{0:T(256)(128)(2,1)S(1)} %fusion) | copy-start | bytes 772
  33.3 0.6 copy-start.1
  34.0 0.6 copy-start.3
  36.0 25.3 %collective-permute-start.6 = (bf16[2,4,136,147]{3,2,1,0:T(8,128)(2,1)}, bf16[2,4,136,147]{3,2,1,0:T(8,128)(2,1)}, u32[]{:S(2)}, u32[]{:S(2)}) collective-permute-start(bf16[2,4,136,147]{3,2,1,0:T(8,128)(2,1)} %get-tuple-element.3), channel_id=1, source_target_pairs={{1,0},{2,1},{3,2},{4,3},{5,4},{6,5},{7,6},{8,7},{9,8},{10,9},{11,1... | collective-permute-start | bytes 959624 | tf_op jit(solution)/shard_map/ppermute | solution.py:40
  38.1 23.5 %collective-permute-start.2 = (bf16[2,4,136,147]{3,2,1,0:T(8,128)(2,1)S(1)}, bf16[2,4,136,147]{3,2,1,0:T(8,128)(2,1)S(1)}, u32[]{:S(2)}, u32[]{:S(2)}) collective-permute-start(bf16[2,4,136,147]{3,2,1,0:T(8,128)(2,1)S(1)} %get-tuple-element.2), channel_id=1, source_target_pairs={{0,1},{1,2},{2,3},{3,4},{4,5},{5,6},{6,7},{7,8},{8,9},{9,10},{10,1... | collective-permute-start | bytes 959624 | tf_op jit(solution)/shard_map/ppermute | solution.py:39
  58.7 2.9 %copy-start.2 = (bf16[2,8,4,147]{3,2,1,0:T(4,128)(2,1)S(1)}, bf16[2,8,4,147]{3,2,1,0:T(4,128)(2,1)}, u32[]{:S(2)}) copy-start(bf16[2,8,4,147]{3,2,1,0:T(4,128)(2,1)} %copy-done.1) | copy-start | bytes 56452
  58.7 2.9 %copy-start.4 = (bf16[2,8,4,147]{3,2,1,0:T(4,128)(2,1)S(1)}, bf16[2,8,4,147]{3,2,1,0:T(4,128)(2,1)}, u32[]{:S(2)}) copy-start(bf16[2,8,4,147]{3,2,1,0:T(4,128)(2,1)} %copy-done.3) | copy-start | bytes 56452
